TPU v7x, 256 devices: a whole 4x4x8 slice. The times are simulated.
256 devices in a mesh: dp: 32 (over y, z), tensor: 8 (over x, core).
Axes of the slice: x: 4, y: 4, z: 8, core: 2. Of those that a mesh axis runs over, the one named last changes fastest.
Arguments:
- residual_in: bfloat16 [2048, 2048], P(('dp', 'tensor')), may hold values from -6 to 6
- attn_gain: float32 [2048], replicated, may hold values from 0.5 to 1.5
- query_weight: bfloat16 [2048, 4096], P(None, 'tensor'), may hold values from -0.125 to 0.125
- kv_weight: bfloat16 [2048, 1024], P(None, 'tensor'), may hold values from -0.125 to 0.125
- query_gain: float32 [128], replicated, may hold values from 0.25 to 1.75
- key_gain: float32 [128], replicated, may hold values from 0.25 to 1.75
- out_weight: bfloat16 [4096, 2048], P('tensor'), may hold values from -0.09375 to 0.09375
- moe_gain: float32 [2048], replicated, may hold values from 0.5 to 1.5
- gate_weight: bfloat16 [128, 2048, 768], P('dp', None, 'tensor'), may hold values from -0.1875 to 0.1875
- lift_weight: bfloat16 [128, 2048, 768], P('dp', None, 'tensor'), may hold values from -0.1875 to 0.1875
- down_weight: bfloat16 [128, 768, 2048], P('dp', 'tensor'), may hold values from -0.21875 to 0.21875
- routes: int32 [2048, 8], P('dp'), may hold values from 0 to 127, as said below
- route_weights: float32 [2048, 8], P('dp'), may hold values from 0.5 to 1
- prefix_cache: bfloat16 [64, 2048, 1024], P('dp', 'tensor'), may hold values from -250 to 250
- suffix_cache: bfloat16 [2048, 128, 1024], P('dp', 'tensor'), may hold values from -250 to 250
- prefix_len: int32 [64], P('dp'), may hold values from 1 to 2048, as said below
- suffix_len: int32 [2048], P('dp'), may hold values from 1 to 128, as said below
- request_group: int32 [2048], P('dp'), may hold values from 0 to 63, as said below
Outputs:
- layer_out: bfloat16 [2048, 2048], P(('dp', 'tensor'))
- new_cache_rows: bfloat16 [2048, 1024], P('dp', 'tensor')
Inputs may be any that keep to these rules, and one draw needn't show every extreme that they name: `routes`: each block of 64 rows (the requests of one index of dp) names 64 of the experts exactly 8 times each and no other expert; one expert is among them in every block. `request_group`: request r belongs to one of the groups (r // 64) * 2 to (r // 64) * 2 + 1. `prefix_len`: some shared prompt has all 2048 slots live. `suffix_len`: some request has all 128 suffix slots live.
All inputs are finite; a program needn't handle non-finite values.
Results may differ from a plain program's by a relative error of at most 0.02.
Values may be sent and summed in bfloat16 or wider, within the bound.
No kernel may reach another device: no remote copies, remote signals or barrier semaphores. Data moves between devices by JAX's collectives and lax.ppermute only.
A program may use at most 128 MiB of HBM per device.

v0:
```python
import math
import jax
import jax.numpy as jnp
from jax import lax
from jax.sharding import PartitionSpec as P

EPSILON = 1e-06
THETA = 1000000.0
NEGATIVE = -1e30


def merged(array, axis, combine):
    everything = jax.tree.map(lambda part: lax.all_gather(part, axis), array)
    first = jax.tree.map(lambda part: part[0], everything)

    def hop(k, so_far):
        return combine(so_far, jax.tree.map(lambda part: part[k], everything))

    return lax.fori_loop(1, lax.axis_size(axis), hop, first)


def rms_scale(values, gain):
    mean_square = jnp.mean(values * values, axis=-1, keepdims=True)
    return values * lax.rsqrt(mean_square + EPSILON) * gain


def rotate(values, positions):
    half = values.shape[-1] // 2
    freqs = THETA ** (-jnp.arange(half).astype(jnp.float32) * 2.0 / values.shape[-1])
    angles = positions.astype(jnp.float32)[:, None] * freqs[None, :]
    angles = jnp.concatenate([angles, angles], axis=-1)
    cosine = jnp.cos(angles)[:, None, :]
    sine = jnp.sin(angles)[:, None, :]
    turned = jnp.concatenate([-values[..., half:], values[..., :half]], axis=-1)
    return values * cosine + turned * sine


def combine_parts(first, second):
    top_first, total_first, sums_first = first
    top_second, total_second, sums_second = second
    top_new = jnp.maximum(top_first, top_second)
    factor_first = jnp.exp(top_first - top_new)
    factor_second = jnp.exp(top_second - top_new)
    return (
        top_new,
        total_first * factor_first + total_second * factor_second,
        sums_first * factor_first[..., None] + sums_second * factor_second[..., None],
    )


def body(
    residual_in,
    attn_gain,
    query_weight,
    kv_weight,
    query_gain,
    key_gain,
    out_weight,
    moe_gain,
    gate_weight,
    lift_weight,
    down_weight,
    routes,
    route_weights,
    prefix_cache,
    suffix_cache,
    prefix_len,
    suffix_len,
    request_group,
):
    tensor_size = lax.axis_size("tensor")
    tensor_rank = lax.axis_index("tensor")
    dp_rank = lax.axis_index("dp")
    owners = lax.axis_size("dp")
    head_dim = query_gain.shape[0]
    requests = routes.shape[0]
    model_width = residual_in.shape[1]
    query_cols = query_weight.shape[1]
    kv_cols = kv_weight.shape[1]
    heads_here = query_cols // head_dim
    heads_all = heads_here * tensor_size
    kv_heads_all = kv_cols * tensor_size // (2 * head_dim)
    per_group = heads_all // kv_heads_all
    groups_dev = prefix_cache.shape[0]
    pre_local = prefix_cache.shape[1]
    suf_local = suffix_cache.shape[1]
    normed = rms_scale(residual_in.astype(jnp.float32), attn_gain).astype(jnp.bfloat16)
    piece = lax.all_gather(normed, "tensor", axis=0, tiled=True)
    projected = jnp.concatenate(
        [
            jnp.dot(piece, query_weight, preferred_element_type=jnp.float32),
            jnp.dot(piece, kv_weight, preferred_element_type=jnp.float32),
        ],
        axis=1,
    )
    query_raw = projected[:, :query_cols].reshape(requests, heads_here, head_dim)
    kv_raw = projected[:, query_cols:].reshape(requests, kv_cols // head_dim, head_dim)
    group_ids = dp_rank * groups_dev + jnp.arange(groups_dev)
    member = request_group[:, None] == group_ids[None, :]
    prefix_of = jnp.sum(jnp.where(member, prefix_len[None, :], 0), axis=1)
    positions = prefix_of + suffix_len
    queries = rotate(rms_scale(query_raw, query_gain), positions).astype(jnp.bfloat16)
    head_number = tensor_rank * (kv_cols // head_dim) + jnp.arange(kv_cols // head_dim)
    is_key = (head_number < kv_heads_all)[None, :, None]
    keyed = rotate(rms_scale(kv_raw, key_gain), positions)
    new_rows = jnp.where(is_key, keyed, kv_raw).astype(jnp.bfloat16).reshape(requests, kv_cols)
    joined = jnp.concatenate([queries.reshape(requests, query_cols), new_rows], axis=1)
    every_head = lax.all_gather(joined, "tensor", axis=1, tiled=True).reshape(
        requests, tensor_size, query_cols + kv_cols
    )
    all_queries = every_head[:, :, :query_cols].reshape(requests, kv_heads_all, per_group, head_dim)
    all_kv = every_head[:, :, query_cols:]
    own_keys = all_kv[:, :kv_heads_all]
    own_values = all_kv[:, kv_heads_all:].astype(jnp.float32)
    scale = 1.0 / math.sqrt(head_dim)
    split_at = kv_heads_all * head_dim
    pre_keys = prefix_cache[:, :, :split_at].reshape(groups_dev, pre_local, kv_heads_all, head_dim)
    pre_values = prefix_cache[:, :, split_at:].reshape(
        groups_dev, pre_local, kv_heads_all, head_dim
    )
    suf_keys = suffix_cache[:, :, :split_at].reshape(requests, suf_local, kv_heads_all, head_dim)
    suf_values = suffix_cache[:, :, split_at:].reshape(requests, suf_local, kv_heads_all, head_dim)
    pre_scores = (
        jnp.einsum("rgqd,npgd->rgqnp", all_queries, pre_keys, preferred_element_type=jnp.float32)
        * scale
    )
    suf_scores = (
        jnp.einsum("rgqd,rsgd->rgqs", all_queries, suf_keys, preferred_element_type=jnp.float32)
        * scale
    )
    own_scores = (
        jnp.einsum("rgqd,rgd->rgq", all_queries, own_keys, preferred_element_type=jnp.float32)
        * scale
    )
    pre_slots = tensor_rank * pre_local + jnp.arange(pre_local)
    pre_valid = (member[:, :, None] & (pre_slots[None, None, :] < prefix_len[None, :, None]))[
        :, None, None, :, :
    ]
    suf_slots = tensor_rank * suf_local + jnp.arange(suf_local)
    suf_valid = (suf_slots[None, :] < suffix_len[:, None])[:, None, None, :]
    own_valid = tensor_rank == 0
    top_pre = jnp.max(jnp.where(pre_valid, pre_scores, NEGATIVE), axis=(3, 4))
    top_suf = jnp.max(jnp.where(suf_valid, suf_scores, NEGATIVE), axis=3)
    top_own = jnp.where(own_valid, own_scores, NEGATIVE)
    top_local = jnp.maximum(jnp.maximum(top_pre, top_suf), top_own)
    pre_weights = jnp.where(pre_valid, jnp.exp(pre_scores - top_local[..., None, None]), 0.0)
    suf_weights = jnp.where(suf_valid, jnp.exp(suf_scores - top_local[..., None]), 0.0)
    own_weights = jnp.where(own_valid, jnp.exp(own_scores - top_local), 0.0)
    total_local = jnp.sum(pre_weights, axis=(3, 4)) + jnp.sum(suf_weights, axis=3) + own_weights
    sums_local = jnp.einsum(
        "rgqnp,npgd->rgqd",
        pre_weights.astype(jnp.bfloat16),
        pre_values,
        preferred_element_type=jnp.float32,
    )
    sums_local = sums_local + jnp.einsum(
        "rgqs,rsgd->rgqd",
        suf_weights.astype(jnp.bfloat16),
        suf_values,
        preferred_element_type=jnp.float32,
    )
    own_low = own_weights.astype(jnp.bfloat16).astype(jnp.float32)
    sums_local = sums_local + own_low[..., None] * own_values[:, :, None, :]
    top_local = top_local.reshape(requests, heads_all)
    total_local = total_local.reshape(requests, heads_all)
    sums_local = sums_local.reshape(requests, heads_all, head_dim)
    top_all, total_all, sums_all = merged(
        (top_local, total_local, sums_local), "tensor", combine_parts
    )
    total_mine = lax.dynamic_slice_in_dim(total_all, tensor_rank * heads_here, heads_here, 1)
    sums_mine = lax.dynamic_slice_in_dim(sums_all, tensor_rank * heads_here, heads_here, 1)
    mixed = sums_mine / total_mine[..., None]
    attn_heads = mixed.reshape(requests, query_cols).astype(jnp.bfloat16)
    attn_out = lax.psum_scatter(
        jnp.dot(attn_heads, out_weight, preferred_element_type=jnp.float32).astype(jnp.bfloat16),
        "tensor",
        scatter_dimension=0,
        tiled=True,
    ).astype(jnp.float32)
    middle = (residual_in.astype(jnp.float32) + attn_out).astype(jnp.bfloat16)
    moe_in = rms_scale(middle.astype(jnp.float32), moe_gain).astype(jnp.bfloat16)
    local_experts = gate_weight.shape[0]
    experts_all = local_experts * owners
    topk = routes.shape[1]
    capacity = 2 * requests * topk // experts_all
    flat_routes = routes.reshape(-1)
    onehot = (flat_routes[:, None] == jnp.arange(experts_all)[None, :]).astype(jnp.int32)
    running = jnp.cumsum(onehot, axis=0)
    slot_of = jnp.sum(onehot * running, axis=1) - 1
    code_of = (flat_routes * capacity + slot_of).reshape(requests, topk)
    code_span = jnp.arange(experts_all * capacity)
    placing = jnp.any(code_of[None, :, :] == code_span[:, None, None], axis=2).astype(jnp.bfloat16)
    share = route_weights / jnp.sum(route_weights, axis=1, keepdims=True)
    placed = jnp.dot(
        placing,
        lax.all_gather(moe_in, "tensor", axis=0, tiled=True),
        preferred_element_type=jnp.float32,
    )
    outgoing = placed.astype(jnp.bfloat16).reshape(owners, local_experts, capacity, model_width)
    rows = lax.all_to_all(outgoing, "dp", split_axis=0, concat_axis=0, tiled=True)
    gate_val = jnp.einsum("necd,edf->necf", rows, gate_weight, preferred_element_type=jnp.float32)
    lift_val = jnp.einsum("necd,edf->necf", rows, lift_weight, preferred_element_type=jnp.float32)
    hidden_units = (jax.nn.silu(gate_val) * lift_val).astype(jnp.bfloat16)
    returned = lax.all_to_all(
        jnp.einsum(
            "necf,efd->necd", hidden_units, down_weight, preferred_element_type=jnp.float32
        ).astype(jnp.bfloat16),
        "dp",
        split_axis=0,
        concat_axis=0,
        tiled=True,
    ).astype(jnp.float32)
    returned = returned.reshape(experts_all * capacity, model_width)
    picked_rows = returned[code_of]
    moe_out = lax.psum_scatter(
        jnp.sum(share[:, :, None] * picked_rows, axis=1).astype(jnp.bfloat16),
        "tensor",
        scatter_dimension=0,
        tiled=True,
    ).astype(jnp.float32)
    layer_out = (middle.astype(jnp.float32) + moe_out).astype(jnp.bfloat16)
    return (layer_out, new_rows)


def solution(mesh):
    in_specs = (
        P(("dp", "tensor"), None),
        P(),
        P(None, "tensor"),
        P(None, "tensor"),
        P(),
        P(),
        P("tensor", None),
        P(),
        P("dp", None, "tensor"),
        P("dp", None, "tensor"),
        P("dp", "tensor", None),
        P("dp", None),
        P("dp", None),
        P("dp", "tensor", None),
        P("dp", "tensor", None),
        P("dp"),
        P("dp"),
        P("dp"),
    )
    out_specs = (P(("dp", "tensor"), None), P("dp", "tensor"))
    return jax.shard_map(body, mesh=mesh, in_specs=in_specs, out_specs=out_specs, check_vma=False)
```

profile of v0, /device:TPU:8, one launch (start us, length us, event | category | flops | bytes accessed | tf_op | source)
XLA Modules:
  0.0 472.5 jit_solution(8575406757492180028)
XLA Ops:
  9.2 13.2 %all_gather.18 = bf16[64,2048]{1,0:T(8,128)(2,1)S(1)} all-gather(bf16[8,2048]{1,0:T(8,128)(2,1)S(1)} %fusion.79), channel_id=1, replica_groups=mesh['dp'=32,'tensor'=8] {'tensor'}, dimensions={0}, use_global_device_ids=true | all-gather | bytes 294912 | tf_op jit(solution)/shard_map/all_gather | solution.py:88
  24.6 2.1 fusion.100
  28.0 13.3 %all_gather.19 = bf16[64,5120]{1,0:T(8,128)(2,1)S(1)} all-gather(bf16[64,640]{1,0:T(8,128)(2,1)S(1)} %pad_maximum_fusion), channel_id=1, replica_groups=mesh['dp'=32,'tensor'=8] {'tensor'}, dimensions={1}, use_global_device_ids=true | all-gather | bytes 737280 | tf_op jit(solution)/shard_map/all_gather | solution.py:108
  42.5 2.1 fusion.98
  44.7 2.0 copy.234
  46.8 4.0 fusion.4
  51.0 3.0 slice_bitcast_fusion.1
  57.2 2.0 fusion.55
  59.2 3.3 fusion.23
  65.2 12.8 %all_gather.20 = f32[8,64,32]{1,2,0:T(8,128)S(1)} all-gather(f32[1,64,32]{1,2,0:T(8,128)S(1)} %bitcast.195), channel_id=1, replica_groups=mesh['dp'=32,'tensor'=8] {'tensor'}, dimensions={0}, use_global_device_ids=true | all-gather | bytes 73728 | tf_op jit(solution)/shard_map/all_gather | solution.py:13
  78.0 4.1 fusion.12
  82.3 13.5 %all_gather.21 = f32[8,64,32]{1,2,0:T(8,128)S(1)} all-gather(f32[1,64,32]{1,2,0:T(8,128)S(1)} %add_bitcast_fusion), channel_id=1, replica_groups=mesh['dp'=32,'tensor'=8] {'tensor'}, dimensions={0}, use_global_device_ids=true | all-gather | bytes 73728 | tf_op jit(solution)/shard_map/all_gather | solution.py:13
  96.7 22.8 %all-gather.2.cloned.1.call-done = f32[8,64,32,128]{3,2,1,0:T(8,128)} async-done(((f32[1,64,32,128]{3,2,1,0:T(8,128)}), f32[8,64,32,128]{3,2,1,0:T(8,128)}) %all-gather.2.cloned.1.call-update) | async-done | bytes 8388624 | tf_op jit(solution)/shard_map/all_gather | solution.py:13
  120.9 20.0 %while.19 = (s32[]{:T(128)}, f32[64,32]{1,0:T(8,128)S(1)}, f32[64,32]{1,0:T(8,128)S(1)}, f32[64,32,128]{2,1,0:T(8,128)S(1)}, f32[8,64,32]{1,2,0:T(8,128)S(1)}, /...) while((s32[]{:T(128)}, f32[64,32]{1,0:T(8,128)S(1)}, ...), condition=%wide.region_9.10_spmd, body=%wide.region_8.9_spmd.sunk | while | flops 798725 | bytes 3293335 | solution.py:19
  121.8 1.9 fusion.114
  124.7 1.9 fusion.114
  127.5 1.9 fusion.114
  130.4 1.9 fusion.114
  133.2 1.9 fusion.114
  138.9 1.9 fusion.114
  143.3 32.8 %reduce-scatter.3.cloned.1.call-done = bf16[8,2048]{1,0:T(8,128)(2,1)} async-done(((bf16[64,2048]{1,0:T(8,128)(2,1)}), bf16[8,2048]{1,0:T(8,128)(2,1)}) %reduce-scatter.3.cloned.1.call-update) | async-done | bytes 32784 | tf_op jit(solution)/shard_map/reduce_scatter | solution.py:174
  177.8 12.8 %all_gather.23 = bf16[64,2048]{1,0:T(8,128)(2,1)S(1)} all-gather(bf16[8,2048]{1,0:T(8,128)(2,1)S(1)} %fusion.83), channel_id=1, replica_groups=mesh['dp'=32,'tensor'=8] {'tensor'}, dimensions={0}, use_global_device_ids=true | all-gather | bytes 294912 | tf_op jit(solution)/shard_map/all_gather | solution.py:196
  192.0 104.1 %all_to_all.10 = bf16[32,4,8,2048]{3,2,1,0:T(8,128)(2,1)S(1)} all-to-all(bf16[32,4,8,2048]{3,2,1,0:T(8,128)(2,1)S(1)} %bitcast.183), channel_id=1, replica_groups=mesh['dp'=32,'tensor'=8] {'dp'}, dimensions={0} | all-to-all | bytes 8388608 | tf_op jit(solution)/shard_map/all_to_all | solution.py:200
  296.1 2.0 copy-done.2
  299.3 7.4 %convert_bitcast_fusion = bf16[32,4,8,2048]{3,2,0,1:T(8,128)(2,1)} fusion(bf16[4,96,2048]{2,1,0:T(8,128)(2,1)} %param.30, bf16[4,2048,96]{1,2,0:T(8,128)(2,1)} %param.29, bf16[32,4,8,2048]{3,2,1,0:T(8,128)(2,1)} %copy-done.2, f32[32,4,8,96]{3,2,0,1:T(8,128)S(1)} %fusion.27), kind=kOutput, calls=%fused_computation.19 | convolution fusion | flops 807993344 | bytes 11927552 | tf_op jit(solution)/shard_map/necf,efd->necd/dot_general | solution.py:205
  306.7 4.7 %copy.211 = bf16[32,4,8,2048]{3,2,1,0:T(8,128)(2,1)} copy(bf16[32,4,8,2048]{3,2,0,1:T(8,128)(2,1)} %convert_bitcast_fusion) | data formatting | bytes 8388608 | tf_op jit(solution)/shard_map/convert_element_type | solution.py:207
  311.4 7.8 %all-to-all-start.1 = ((bf16[32,4,8,2048]{3,2,1,0:T(8,128)(2,1)}), bf16[32,4,8,2048]{3,2,1,0:T(8,128)(2,1)}, u32[]{:S(2)}, u32[]{:S(2)}) async-start(bf16[32,4,8,2048]{3,2,1,0:T(8,128)(2,1)} %copy.211), calls=%async_computation.2 | async-start | bytes 8388608 | tf_op jit(solution)/shard_map/all_to_all | solution.py:204
  319.8 93.7 %all-to-all-done.1 = bf16[32,4,8,2048]{3,2,1,0:T(8,128)(2,1)} async-done(((bf16[32,4,8,2048]{3,2,1,0:T(8,128)(2,1)}), bf16[32,4,8,2048]{3,2,1,0:T(8,128)(2,1)}, u32[]{:S(2)}, u32[]{:S(2)}) %all-to-all-start.1) | async-done | bytes 4194336 | tf_op jit(solution)/shard_map/all_to_all | solution.py:204
  413.5 6.5 %bitcast_convert_fusion = f32[1024,2048]{1,0:T(8,128)} fusion(bf16[32,4,8,2048]{3,2,1,0:T(8,128)(2,1)} %all-to-all-done.1), kind=kLoop, calls=%fused_computation.11 | loop fusion | flops 2097152 | bytes 12582912 | tf_op jit(solution)/shard_map/reshape | solution.py:213
  419.9 8.9 %gather_fusion = f32[512,2048]{1,0:T(8,128)} fusion(f32[1024,2048]{1,0:T(8,128)} %bitcast_convert_fusion, s32[1024]{0:T(1024)S(1)} %pad_clamp_fusion), kind=kCustom, calls=%fused_computation | custom fusion | bytes 8390656 | tf_op jit(solution)/shard_map/gather | solution.py:214
  428.8 4.3 fusion.3
  433.2 31.4 %reduce-scatter.5.cloned.1.call-done = bf16[8,2048]{1,0:T(8,128)(2,1)} async-done(((bf16[64,2048]{1,0:T(8,128)(2,1)}), bf16[8,2048]{1,0:T(8,128)(2,1)}) %reduce-scatter.5.cloned.1.call-update) | async-done | bytes 32784 | tf_op jit(solution)/shard_map/reduce_scatter | solution.py:215
  (164 shorter events, 32.0 us)
Async XLA Ops:
  7.2 133.9 %copy-start = (bf16[512,2048]{1,0:T(8,128)(2,1)S(1)}, bf16[512,2048]{1,0:T(8,128)(2,1)}, u32[]{:S(2)}) copy-start(bf16[512,2048]{1,0:T(8,128)(2,1)} %param.26) | copy-start | bytes 6291460
  7.2 20.3 %copy-start.15 = (f32[128]{0:T(128)S(1)}, f32[128]{0:T(128)}, u32[]{:S(2)}) copy-start(f32[128]{0:T(128)} %param.25) | copy-start | bytes 1540
  7.2 19.7 %copy-start.16 = (f32[128]{0:T(128)S(1)}, f32[128]{0:T(128)}, u32[]{:S(2)}) copy-start(f32[128]{0:T(128)} %param.24) | copy-start | bytes 1540
  7.2 20.0 %copy-start.18 = (s32[2]{0:T(128)S(1)}, s32[2]{0:T(128)}, u32[]{:S(2)}) copy-start(s32[2]{0:T(128)} %param.35) | copy-start | bytes 28
  7.2 20.0 %copy-start.17 = (s32[64]{0:T(128)S(1)}, s32[64]{0:T(128)}, u32[]{:S(2)}) copy-start(s32[64]{0:T(128)} %param.37) | copy-start | bytes 772
  7.2 20.1 %copy-start.19 = (s32[64]{0:T(128)S(1)}, s32[64]{0:T(128)}, u32[]{:S(2)}) copy-start(s32[64]{0:T(128)} %param.36) | copy-start | bytes 772
  7.2 112.3 %all-gather.2.cloned.1.call-start = ((), (), s32[]{:S(2)}) async-start(), calls=%async_computation.4 | async-start | bytes 9437184 | tf_op jit(solution)/shard_map/all_gather | solution.py:13
  27.7 13.7 %copy-start.9 = (bf16[64,128]{1,0:T(8,128)(2,1)}, bf16[64,128]{1,0:T(8,128)(2,1)S(1)}, u32[]{:S(2)}) copy-start(bf16[64,128]{1,0:T(8,128)(2,1)S(1)} %get-tuple-element.258) | copy-start | bytes 49156
  42.5 13.3 %copy-start.7 = (f32[64,4,1,8]{0,3,1,2:T(8,128)}, f32[64,4,1,8]{0,3,1,2:T(8,128)S(1)}, u32[]{:S(2)}) copy-start(f32[64,4,1,8]{0,3,1,2:T(8,128)S(1)} %copy.216) | copy-start | bytes 24580
  57.1 5.4 %copy-start.3 = (bf16[64,2,4,8,128]{4,3,2,1,0:T(8,128)(2,1)S(1)}, bf16[64,2,4,8,128]{4,3,2,1,0:T(8,128)(2,1)}, u32[]{:S(2)}) copy-start(bf16[64,2,4,8,128]{4,3,2,1,0:T(8,128)(2,1)} %get-tuple-element.247) | copy-start | bytes 3145732
  62.5 1.9 copy-start.11
  64.4 17.9 %copy-start.8 = (f32[64,4,1,8]{0,3,1,2:T(8,128)S(1)}, f32[64,4,1,8]{0,3,1,2:T(8,128)}, u32[]{:S(2)}) copy-start(f32[64,4,1,8]{0,3,1,2:T(8,128)} %copy-done.7) | copy-start | bytes 24580
  64.4 111.7 %reduce-scatter.3.cloned.1.call-start = ((), (), s32[]{:S(2)}) async-start(), calls=%async_computation.5 | async-start | bytes 294912 | tf_op jit(solution)/shard_map/reduce_scatter | solution.py:174
  95.8 25.0 %copy-start.5 = (f32[8,64,32]{1,2,0:T(8,128)}, f32[8,64,32]{1,2,0:T(8,128)S(1)}, u32[]{:S(2)}) copy-start(f32[8,64,32]{1,2,0:T(8,128)S(1)} %all_gather.21) | copy-start | bytes 196612
  120.8 21.5 %copy-start.13 = (s32[512]{0:T(512)S(1)}, s32[512]{0:T(512)}, u32[]{:S(2)}) copy-start(s32[512]{0:T(512)} %fusion.67) | copy-start | bytes 6148
  120.8 21.6 %copy-start.12 = (s32[64,8]{0,1:T(8,128)S(1)}, s32[64,8]{0,1:T(8,128)}, u32[]{:S(2)}) copy-start(s32[64,8]{0,1:T(8,128)} %param.31) | copy-start | bytes 6148
  120.8 55.3 %copy-start.4 = (bf16[8,2048]{1,0:T(8,128)(2,1)S(1)}, bf16[8,2048]{1,0:T(8,128)(2,1)}, u32[]{:S(2)}) copy-start(bf16[8,2048]{1,0:T(8,128)(2,1)} %param.20) | copy-start | bytes 98308
  120.8 56.2 %copy-start.14 = (f32[2048]{0:T(1024)S(1)}, f32[2048]{0:T(1024)}, u32[]{:S(2)}) copy-start(f32[2048]{0:T(1024)} %param.27) | copy-start | bytes 24580
  192.0 106.1 %copy-start.20 = (bf16[4,2048,96]{1,2,0:T(8,128)(2,1)S(1)}, bf16[4,2048,96]{1,2,0:T(8,128)(2,1)}, u32[]{:S(2)}) copy-start(bf16[4,2048,96]{1,2,0:T(8,128)(2,1)} %param.28) | copy-start | bytes 4718596
  296.1 2.0 copy-start.2
  311.4 8.2 %copy-start.10 = (f32[64,8]{0,1:T(8,128)S(1)}, f32[64,8]{0,1:T(8,128)}, u32[]{:S(2)}) copy-start(f32[64,8]{0,1:T(8,128)} %param.32) | copy-start | bytes 6148
  311.4 102.0 %all-to-all-start.1 = ((bf16[32,4,8,2048]{3,2,1,0:T(8,128)(2,1)}), bf16[32,4,8,2048]{3,2,1,0:T(8,128)(2,1)}, u32[]{:S(2)}, u32[]{:S(2)}) async-start(bf16[32,4,8,2048]{3,2,1,0:T(8,128)(2,1)} %copy.211), calls=%async_computation.2 | async-start | bytes 8388608 | tf_op jit(solution)/shard_map/all_to_all | solution.py:204
  319.2 145.4 %reduce-scatter.5.cloned.1.call-start = ((), (), s32[]{:S(2)}) async-start(), calls=%async_computation.6 | async-start | bytes 294912 | tf_op jit(solution)/shard_map/reduce_scatter | solution.py:215
  419.9 46.1 %copy-start.1 = (bf16[512,2048]{1,0:T(8,128)(2,1)S(1)}, bf16[512,2048]{1,0:T(8,128)(2,1)}, u32[]{:S(2)}) copy-start(bf16[512,2048]{1,0:T(8,128)(2,1)} %param.26) | copy-start | bytes 6291460
  428.8 35.8 %copy-start.6 = (bf16[8,2048]{1,0:T(8,128)(2,1)S(1)}, bf16[8,2048]{1,0:T(8,128)(2,1)}, u32[]{:S(2)}) copy-start(bf16[8,2048]{1,0:T(8,128)(2,1)} %reduce-scatter.3.cloned.1.call-done) | copy-start | bytes 98308
Sparse Core Ops, SparseCore 0:
  64.5 54.9 all-gather.1
  142.4 33.6 reduce-scatter.2
  433.3 31.2 reduce-scatter.4
where the time goes:
time: 474 us; the launch traced here: 473 us
  waiting for transfers between devices  181 us (38%)
  blocking collectives  170 us (36%)
  other arithmetic  39.7 us (8%)
  local copies, waits for them, and re-layouts  35.1 us (7%)
  matrix products  24.6 us (5%)
  between operations  14.3 us (3%)
  starting transfers between devices  8.12 us (2%)
    all_to_all x1, blocking collectives, body(): lax.all_to_all(outgoing, 'dp', split_axis=0, concat_axis=0, tiled=True)  104 us
    all_to_all x1, waiting for transfers between devices, body(): lax.all_to_all(jnp.einsum('necf,efd->necd', hidden_units, down_weight, pr...  93.7 us
    reduce_scatter x1, waiting for transfers between devices, body(): lax.psum_scatter(jnp.dot(attn_heads, out_weight, preferred_element_type=j...  32.8 us
    reduce_scatter x1, waiting for transfers between devices, body(): lax.psum_scatter(jnp.sum(share[:, :, None] * picked_rows, axis=1).astype(...  31.4 us
    all_gather x2, blocking collectives, merged(): everything = jax.tree.map(lambda part: lax.all_gather(part, axis), array)  26.3 us
    all_gather x1, waiting for transfers between devices, merged(): everything = jax.tree.map(lambda part: lax.all_gather(part, axis), array)  22.8 us
    all_gather x1, blocking collectives, body(): lax.all_gather(joined, 'tensor', axis=1, tiled=True)  13.3 us
    add x7, other arithmetic, combine_parts(): sums_first * factor_first[..., None]  13.3 us
  transfers between devices with their start and end apart: 4, of which 4 were waited for; matrix products, arithmetic and copies ran while one was open for 2% of the time, Pallas kernels for 0%

commit v1 on v0

--- a/solution.py
+++ b/solution.py
@@ -7,6 +7,12 @@
 EPSILON = 1e-06
 THETA = 1000000.0
 NEGATIVE = -1e30
+use_ratios_here = lambda in_array, mesh_name, dim_at: jnp.concatenate(
+    jax.lax.all_to_all(
+        jnp.stack([in_array for _ in range(jax.lax.axis_size(mesh_name))]), mesh_name, 0, 0
+    ),
+    axis=dim_at,
+)
 
 
 def merged(array, axis, combine):
@@ -192,9 +198,7 @@
     placing = jnp.any(code_of[None, :, :] == code_span[:, None, None], axis=2).astype(jnp.bfloat16)
     share = route_weights / jnp.sum(route_weights, axis=1, keepdims=True)
     placed = jnp.dot(
-        placing,
-        lax.all_gather(moe_in, "tensor", axis=0, tiled=True),
-        preferred_element_type=jnp.float32,
+        placing, use_ratios_here(moe_in, "tensor", 0), preferred_element_type=jnp.float32
     )
     outgoing = placed.astype(jnp.bfloat16).reshape(owners, local_experts, capacity, model_width)
     rows = lax.all_to_all(outgoing, "dp", split_axis=0, concat_axis=0, tiled=True)

time: 474 us -> 471 us (level)
  blocking collectives: 170 us -> 156 us
    all_gather x1 -> x0, blocking collectives: 12.8 us -> none  [body(): lax.all_gather(moe_in, 'tensor', axis=0, tiled=True)]
    all_to_all x0 -> x1, waiting for transfers between devices: none -> 6.62 us  [jax.lax.all_to_all(jnp.stack([in_array for _ in range(jax.lax.axis_size(m...]
  transfers between devices with their start and end apart: 4 -> 5, of which waited for: 4 -> 5; matrix products, arithmetic and copies ran while one was open for 2% -> 2% of each run, Pallas kernels for 0% -> 0%
where the time goes in v1:
time: 471 us; the launch traced here: 469 us
  waiting for transfers between devices  184 us (39%)
  blocking collectives  156 us (33%)
  other arithmetic  40 us (8%)
  local copies, waits for them, and re-layouts  38.9 us (8%)
  matrix products  24.6 us (5%)
  between operations  14.3 us (3%)
  starting transfers between devices  11.4 us (2%)
    all_to_all x1, blocking collectives, body(): lax.all_to_all(outgoing, 'dp', split_axis=0, concat_axis=0, tiled=True)  103 us
    all_to_all x1, waiting for transfers between devices, body(): lax.all_to_all(jnp.einsum('necf,efd->necd', hidden_units, down_weight, pr...  92.4 us
    reduce_scatter x1, waiting for transfers between devices, body(): lax.psum_scatter(jnp.dot(attn_heads, out_weight, preferred_element_type=j...  32.1 us
    reduce_scatter x1, waiting for transfers between devices, body(): lax.psum_scatter(jnp.sum(share[:, :, None] * picked_rows, axis=1).astype(...  31.6 us
    all_gather x2, blocking collectives, merged(): everything = jax.tree.map(lambda part: lax.all_gather(part, axis), array)  26.3 us
    all_gather x1, waiting for transfers between devices, merged(): everything = jax.tree.map(lambda part: lax.all_gather(part, axis), array)  21 us
    all_gather x1, blocking collectives, body(): lax.all_gather(joined, 'tensor', axis=1, tiled=True)  13.3 us
    add x7, other arithmetic, combine_parts(): sums_first * factor_first[..., None]  13.3 us
  transfers between devices with their start and end apart: 5, of which 5 were waited for; matrix products, arithmetic and copies ran while one was open for 2% of the time, Pallas kernels for 0%

profile of v1, /device:TPU:8, one launch (start us, length us, event | category | flops | bytes accessed | tf_op | source)
XLA Modules:
  0.0 469.5 jit_solution(3126423623912691701)
XLA Ops:
  9.2 13.2 %all_gather.15 = bf16[64,2048]{1,0:T(8,128)(2,1)S(1)} all-gather(bf16[8,2048]{1,0:T(8,128)(2,1)S(1)} %fusion.80), channel_id=1, replica_groups=mesh['dp'=32,'tensor'=8] {'tensor'}, dimensions={0}, use_global_device_ids=true | all-gather | bytes 294912 | tf_op jit(solution)/shard_map/all_gather | solution.py:94
  24.6 2.1 fusion.101
  28.0 13.3 %all_gather.16 = bf16[64,5120]{1,0:T(8,128)(2,1)S(1)} all-gather(bf16[64,640]{1,0:T(8,128)(2,1)S(1)} %pad_maximum_fusion), channel_id=1, replica_groups=mesh['dp'=32,'tensor'=8] {'tensor'}, dimensions={1}, use_global_device_ids=true | all-gather | bytes 737280 | tf_op jit(solution)/shard_map/all_gather | solution.py:114
  42.5 2.1 fusion.99
  44.7 2.0 copy.234
  46.8 4.0 fusion.4
  51.0 3.0 slice_bitcast_fusion.1
  57.2 2.0 fusion.55
  59.2 3.3 fusion.23
  66.2 12.7 %all_gather.17 = f32[8,64,32]{1,2,0:T(8,128)S(1)} all-gather(f32[1,64,32]{1,2,0:T(8,128)S(1)} %bitcast.197), channel_id=1, replica_groups=mesh['dp'=32,'tensor'=8] {'tensor'}, dimensions={0}, use_global_device_ids=true | all-gather | bytes 73728 | tf_op jit(solution)/shard_map/all_gather | solution.py:19
  79.7 4.4 fusion.12
  84.2 13.5 %all_gather.18 = f32[8,64,32]{1,2,0:T(8,128)S(1)} all-gather(f32[1,64,32]{1,2,0:T(8,128)S(1)} %add_bitcast_fusion), channel_id=1, replica_groups=mesh['dp'=32,'tensor'=8] {'tensor'}, dimensions={0}, use_global_device_ids=true | all-gather | bytes 73728 | tf_op jit(solution)/shard_map/all_gather | solution.py:19
  98.5 21.0 %all-gather.2.cloned.1.call-done = f32[8,64,32,128]{3,2,1,0:T(8,128)} async-done(((f32[1,64,32,128]{3,2,1,0:T(8,128)}), f32[8,64,32,128]{3,2,1,0:T(8,128)}) %all-gather.2.cloned.1.call-update) | async-done | bytes 8388624 | tf_op jit(solution)/shard_map/all_gather | solution.py:19
  120.8 20.1 %while.19 = (s32[]{:T(128)}, f32[64,32]{1,0:T(8,128)S(1)}, f32[64,32]{1,0:T(8,128)S(1)}, f32[64,32,128]{2,1,0:T(8,128)S(1)}, f32[8,64,32]{1,2,0:T(8,128)}, /*ind...) while((s32[]{:T(128)}, f32[64,32]{1,0:T(8,128)S(1)}, ...), condition=%wide.region_9.10_spmd, body=%wide.region_8.9_spmd.sunk | while | flops 798725 | bytes 3293335 | solution.py:25
  121.8 1.9 fusion.114
  124.6 1.9 fusion.114
  127.5 1.9 fusion.114
  133.3 1.9 fusion.114
  139.0 1.9 fusion.114
  144.1 32.1 %reduce-scatter.3.cloned.1.call-done = bf16[8,2048]{1,0:T(8,128)(2,1)} async-done(((bf16[64,2048]{1,0:T(8,128)(2,1)}), bf16[8,2048]{1,0:T(8,128)(2,1)}) %reduce-scatter.3.cloned.1.call-update) | async-done | bytes 32784 | tf_op jit(solution)/shard_map/reduce_scatter | solution.py:180
  178.7 3.4 all-to-all-start
  182.9 6.6 %all-to-all-done = bf16[8,8,2048]{2,1,0:T(8,128)(2,1)S(1)} async-done(((bf16[8,8,2048]{2,1,0:T(8,128)(2,1)}), bf16[8,8,2048]{2,1,0:T(8,128)(2,1)S(1)}, u32[]{:S(2)}, u32[]{:S(2)}) %all-to-all-start) | async-done | bytes 262176 | tf_op jit(solution)/shard_map/all_to_all | solution.py:11
  190.8 103.4 %all_to_all.15 = bf16[32,4,8,2048]{3,2,1,0:T(8,128)(2,1)S(1)} all-to-all(bf16[32,4,8,2048]{3,2,1,0:T(8,128)(2,1)S(1)} %bitcast.185), channel_id=1, replica_groups=mesh['dp'=32,'tensor'=8] {'dp'}, dimensions={0} | all-to-all | bytes 8388608 | tf_op jit(solution)/shard_map/all_to_all | solution.py:204
  294.2 2.0 copy-done.2
  297.4 7.4 %convert_bitcast_fusion = bf16[32,4,8,2048]{3,2,0,1:T(8,128)(2,1)} fusion(bf16[4,96,2048]{2,1,0:T(8,128)(2,1)} %param.30, bf16[4,2048,96]{1,2,0:T(8,128)(2,1)} %param.29, bf16[32,4,8,2048]{3,2,1,0:T(8,128)(2,1)} %copy-done.2, f32[32,4,8,96]{3,2,0,1:T(8,128)S(1)} %fusion.27), kind=kOutput, calls=%fused_computation.19 | convolution fusion | flops 807993344 | bytes 11927552 | tf_op jit(solution)/shard_map/necf,efd->necd/dot_general | solution.py:209
  304.8 4.7 %copy.211 = bf16[32,4,8,2048]{3,2,1,0:T(8,128)(2,1)} copy(bf16[32,4,8,2048]{3,2,0,1:T(8,128)(2,1)} %convert_bitcast_fusion) | data formatting | bytes 8388608 | tf_op jit(solution)/shard_map/convert_element_type | solution.py:211
  309.5 7.7 %all-to-all-start.2 = ((bf16[32,4,8,2048]{3,2,1,0:T(8,128)(2,1)}), bf16[32,4,8,2048]{3,2,1,0:T(8,128)(2,1)}, u32[]{:S(2)}, u32[]{:S(2)}) async-start(bf16[32,4,8,2048]{3,2,1,0:T(8,128)(2,1)} %copy.211), calls=%async_computation.3 | async-start | bytes 8388608 | tf_op jit(solution)/shard_map/all_to_all | solution.py:208
  317.8 92.4 %all-to-all-done.2 = bf16[32,4,8,2048]{3,2,1,0:T(8,128)(2,1)} async-done(((bf16[32,4,8,2048]{3,2,1,0:T(8,128)(2,1)}), bf16[32,4,8,2048]{3,2,1,0:T(8,128)(2,1)}, u32[]{:S(2)}, u32[]{:S(2)}) %all-to-all-start.2) | async-done | bytes 4194336 | tf_op jit(solution)/shard_map/all_to_all | solution.py:208
  410.2 6.5 %bitcast_convert_fusion = f32[1024,2048]{1,0:T(8,128)} fusion(bf16[32,4,8,2048]{3,2,1,0:T(8,128)(2,1)} %all-to-all-done.2), kind=kLoop, calls=%fused_computation.11 | loop fusion | flops 2097152 | bytes 12582912 | tf_op jit(solution)/shard_map/reshape | solution.py:217
  416.7 8.9 %gather_fusion = f32[512,2048]{1,0:T(8,128)} fusion(f32[1024,2048]{1,0:T(8,128)} %bitcast_convert_fusion, s32[1024]{0:T(1024)S(1)} %pad_clamp_fusion), kind=kCustom, calls=%fused_computation | custom fusion | bytes 8390656 | tf_op jit(solution)/shard_map/gather | solution.py:218
  425.6 4.3 fusion.3
  429.9 31.6 %reduce-scatter.5.cloned.1.call-done = bf16[8,2048]{1,0:T(8,128)(2,1)} async-done(((bf16[64,2048]{1,0:T(8,128)(2,1)}), bf16[8,2048]{1,0:T(8,128)(2,1)}) %reduce-scatter.5.cloned.1.call-update) | async-done | bytes 32784 | tf_op jit(solution)/shard_map/reduce_scatter | solution.py:219
  (166 shorter events, 37.8 us)
Async XLA Ops:
  7.2 134.0 %copy-start = (bf16[512,2048]{1,0:T(8,128)(2,1)S(1)}, bf16[512,2048]{1,0:T(8,128)(2,1)}, u32[]{:S(2)}) copy-start(bf16[512,2048]{1,0:T(8,128)(2,1)} %param.26) | copy-start | bytes 6291460
  7.2 20.3 %copy-start.15 = (f32[128]{0:T(128)S(1)}, f32[128]{0:T(128)}, u32[]{:S(2)}) copy-start(f32[128]{0:T(128)} %param.25) | copy-start | bytes 1540
  7.2 19.7 %copy-start.16 = (f32[128]{0:T(128)S(1)}, f32[128]{0:T(128)}, u32[]{:S(2)}) copy-start(f32[128]{0:T(128)} %param.24) | copy-start | bytes 1540
  7.2 20.0 %copy-start.18 = (s32[2]{0:T(128)S(1)}, s32[2]{0:T(128)}, u32[]{:S(2)}) copy-start(s32[2]{0:T(128)} %param.35) | copy-start | bytes 28
  7.2 20.0 %copy-start.17 = (s32[64]{0:T(128)S(1)}, s32[64]{0:T(128)}, u32[]{:S(2)}) copy-start(s32[64]{0:T(128)} %param.37) | copy-start | bytes 772
  7.2 20.1 %copy-start.19 = (s32[64]{0:T(128)S(1)}, s32[64]{0:T(128)}, u32[]{:S(2)}) copy-start(s32[64]{0:T(128)} %param.36) | copy-start | bytes 772
  7.2 112.3 %all-gather.2.cloned.1.call-start = ((), (), s32[]{:S(2)}) async-start(), calls=%async_computation.5 | async-start | bytes 9437184 | tf_op jit(solution)/shard_map/all_gather | solution.py:19
  27.7 13.7 %copy-start.10 = (bf16[64,128]{1,0:T(8,128)(2,1)}, bf16[64,128]{1,0:T(8,128)(2,1)S(1)}, u32[]{:S(2)}) copy-start(bf16[64,128]{1,0:T(8,128)(2,1)S(1)} %get-tuple-element.258) | copy-start | bytes 49156
  42.5 13.3 %copy-start.8 = (f32[64,4,1,8]{0,3,1,2:T(8,128)}, f32[64,4,1,8]{0,3,1,2:T(8,128)S(1)}, u32[]{:S(2)}) copy-start(f32[64,4,1,8]{0,3,1,2:T(8,128)S(1)} %copy.216) | copy-start | bytes 24580
  57.1 5.4 %copy-start.3 = (bf16[64,2,4,8,128]{4,3,2,1,0:T(8,128)(2,1)S(1)}, bf16[64,2,4,8,128]{4,3,2,1,0:T(8,128)(2,1)}, u32[]{:S(2)}) copy-start(bf16[64,2,4,8,128]{4,3,2,1,0:T(8,128)(2,1)} %get-tuple-element.247) | copy-start | bytes 3145732
  62.5 2.0 copy-start.12
  63.2 21.0 %copy-start.9 = (f32[64,4,1,8]{0,3,1,2:T(8,128)S(1)}, f32[64,4,1,8]{0,3,1,2:T(8,128)}, u32[]{:S(2)}) copy-start(f32[64,4,1,8]{0,3,1,2:T(8,128)} %copy-done.8) | copy-start | bytes 24580
  64.4 111.8 %reduce-scatter.3.cloned.1.call-start = ((), (), s32[]{:S(2)}) async-start(), calls=%async_computation.6 | async-start | bytes 294912 | tf_op jit(solution)/shard_map/reduce_scatter | solution.py:180
  78.9 0.7 copy-start.5
  97.7 0.7 copy-start.6
  140.9 35.3 %copy-start.4 = (bf16[8,2048]{1,0:T(8,128)(2,1)S(1)}, bf16[8,2048]{1,0:T(8,128)(2,1)}, u32[]{:S(2)}) copy-start(bf16[8,2048]{1,0:T(8,128)(2,1)} %param.20) | copy-start | bytes 98308
  140.9 41.1 %copy-start.13 = (s32[64,8]{0,1:T(8,128)S(1)}, s32[64,8]{0,1:T(8,128)}, u32[]{:S(2)}) copy-start(s32[64,8]{0,1:T(8,128)} %param.31) | copy-start | bytes 6148
  141.0 36.1 %copy-start.14 = (f32[2048]{0:T(1024)S(1)}, f32[2048]{0:T(1024)}, u32[]{:S(2)}) copy-start(f32[2048]{0:T(1024)} %param.27) | copy-start | bytes 24580
  178.7 10.8 %all-to-all-start = ((bf16[8,8,2048]{2,1,0:T(8,128)(2,1)}), bf16[8,8,2048]{2,1,0:T(8,128)(2,1)S(1)}, u32[]{:S(2)}, u32[]{:S(2)}) async-start(bf16[8,8,2048]{2,1,0:T(8,128)(2,1)} %stack.2), calls=%async_computation.1 | async-start | bytes 524288 | tf_op jit(solution)/shard_map/all_to_all | solution.py:11
  190.8 105.4 %copy-start.20 = (bf16[4,2048,96]{1,2,0:T(8,128)(2,1)S(1)}, bf16[4,2048,96]{1,2,0:T(8,128)(2,1)}, u32[]{:S(2)}) copy-start(bf16[4,2048,96]{1,2,0:T(8,128)(2,1)} %param.28) | copy-start | bytes 4718596
  294.2 2.0 copy-start.2
  309.5 8.1 %copy-start.11 = (f32[64,8]{0,1:T(8,128)S(1)}, f32[64,8]{0,1:T(8,128)}, u32[]{:S(2)}) copy-start(f32[64,8]{0,1:T(8,128)} %param.32) | copy-start | bytes 6148
  309.5 100.6 %all-to-all-start.2 = ((bf16[32,4,8,2048]{3,2,1,0:T(8,128)(2,1)}), bf16[32,4,8,2048]{3,2,1,0:T(8,128)(2,1)}, u32[]{:S(2)}, u32[]{:S(2)}) async-start(bf16[32,4,8,2048]{3,2,1,0:T(8,128)(2,1)} %copy.211), calls=%async_computation.3 | async-start | bytes 8388608 | tf_op jit(solution)/shard_map/all_to_all | solution.py:208
  317.2 144.3 %reduce-scatter.5.cloned.1.call-start = ((), (), s32[]{:S(2)}) async-start(), calls=%async_computation.7 | async-start | bytes 294912 | tf_op jit(solution)/shard_map/reduce_scatter | solution.py:219
  416.7 46.3 %copy-start.1 = (bf16[512,2048]{1,0:T(8,128)(2,1)S(1)}, bf16[512,2048]{1,0:T(8,128)(2,1)}, u32[]{:S(2)}) copy-start(bf16[512,2048]{1,0:T(8,128)(2,1)} %param.26) | copy-start | bytes 6291460
  425.6 36.0 %copy-start.7 = (bf16[8,2048]{1,0:T(8,128)(2,1)S(1)}, bf16[8,2048]{1,0:T(8,128)(2,1)}, u32[]{:S(2)}) copy-start(bf16[8,2048]{1,0:T(8,128)(2,1)} %reduce-scatter.3.cloned.1.call-done) | copy-start | bytes 98308
Sparse Core Ops, SparseCore 0:
  64.5 54.9 all-gather.1
  142.5 33.6 reduce-scatter.2
  430.1 31.4 reduce-scatter.4
